TPU v7x, 128 devices: a whole 4x4x4 slice. The times are simulated.
128 devices in a mesh: req: 16 (over z, x), mlp: 8 (over y, core).
Axes of the slice: x: 4, y: 4, z: 4, core: 2. Of those that a mesh axis runs over, the one named last changes fastest.
Arguments:
- residual_input: bfloat16 [9216, 5120], P('req', 'mlp'), as said below
- attention_output: bfloat16 [9216, 3072], P('req', 'mlp'), may hold values from -6 to 6
- request_length: int32 [16, 4], replicated, may hold values from 1 to 573, as said below
- request_group: int32 [64], replicated, may hold values from 0 to 7
- adapter_per_group: int32 [8], replicated, may hold values from 0 to 15
- output_weight: bfloat16 [3072, 5120], P('mlp', 'req'), may hold values from -0.109375 to 0.109375
- output_down_maps: bfloat16 [3072, 16, 16], P('mlp'), may hold values from -0.109375 to 0.109375
- output_up_maps: bfloat16 [16, 16, 5120], P(None, None, 'mlp'), may hold values from -1.5 to 1.5
- modulation: float32 [8, 3, 5120], replicated, may hold values from -3 to 3
- hidden_down_maps: bfloat16 [5120, 16, 16], P('mlp'), may hold values from -0.078125 to 0.078125
- hidden_up_maps: bfloat16 [16, 16, 6912], P(None, None, 'mlp'), may hold values from -1.5 to 1.5
- up_weight: bfloat16 [5120, 6912], P('req', 'mlp'), may hold values from -0.078125 to 0.078125
- down_weight: bfloat16 [6912, 5120], P('mlp', 'req'), may hold values from -0.078125 to 0.078125
Outputs:
- layer_out: bfloat16 [384, 16, 5120], P(None, 'req', 'mlp')
Inputs may be any that keep to these rules, and one draw needn't show every extreme that they name: `request_length`: the 4 lengths of one block sum to at most 576, and to exactly 576 for one block; all lengths together sum to 6144. One request has exactly the largest length. `residual_input`: rows of a block past its live rows are never read.
All inputs are finite; a program needn't handle non-finite values.
Results may differ from a plain program's by a relative error of at most 0.012.
Values may be sent and summed in bfloat16 or wider, within the bound.
No kernel may reach another device: no remote copies, remote signals or barrier semaphores. Data moves between devices by JAX's collectives and lax.ppermute only.
A program may use at most 192 MiB of HBM per device.

v0:
```python
import jax
import jax.numpy as jnp
from jax import lax
from jax.sharding import PartitionSpec as P

MODEL_WIDTH = 5120
ADAPTER_RANK = 16
ADAPTER_TOTAL = 16
TOK_DEV = 384
CAP = 576
norm_epsilon = 1e-06


def send_layout(packed, offset, req_count):
    shaped = packed.reshape(packed.shape[0] // req_count, req_count, packed.shape[1])
    return jnp.roll(shaped, offset, axis=1)


def compact(moved, starts, ends, req_count, device_index):
    slots = moved.shape[0] * moved.shape[1]
    flat_rows = moved.reshape(slots, moved.shape[2])
    token_rank = jnp.arange(TOK_DEV, dtype=jnp.int32) * req_count + device_index
    source = jnp.sum((ends[None, :] <= token_rank[:, None]).astype(jnp.int32), axis=1)
    source_hot = source[:, None] == jnp.arange(req_count, dtype=jnp.int32)[None, :]
    source_start = jnp.sum(jnp.where(source_hot, starts[None, :], 0), axis=1)
    position = (token_rank - source_start) // req_count * req_count + source
    return jnp.take(flat_rows, position, axis=0)


def token_tables(token_rank, request_length, request_group, adapter_per_group, modulation):
    req_ends = jnp.cumsum(request_length.reshape(-1))
    request_count = req_ends.shape[0]
    request = jnp.sum((req_ends[None, :] <= token_rank[:, None]).astype(jnp.int32), axis=1)
    request = jnp.minimum(request, request_count - 1)
    request_hot = request[:, None] == jnp.arange(request_count, dtype=jnp.int32)[None, :]
    group_ids = jnp.sum(jnp.where(request_hot, request_group[None, :], 0), axis=1)
    group_count = adapter_per_group.shape[0]
    group_hot = group_ids[:, None] == jnp.arange(group_count, dtype=jnp.int32)[None, :]
    adapter_of_row = jnp.sum(jnp.where(group_hot, adapter_per_group[None, :], 0), axis=1)
    adapter_hot = (
        adapter_of_row[:, None] == jnp.arange(ADAPTER_TOTAL, dtype=jnp.int32)[None, :]
    ).astype(jnp.float32)
    mod_rows = jnp.dot(
        group_hot.astype(jnp.float32),
        modulation.reshape(group_count, -1),
        precision=lax.Precision.HIGHEST,
    )
    return (adapter_hot, mod_rows.reshape(token_rank.shape[0], 3, modulation.shape[2]))


def select_low(output_rank_rows, adapter_hot):
    shaped = output_rank_rows.reshape(output_rank_rows.shape[0], ADAPTER_TOTAL, ADAPTER_RANK)
    return jnp.sum(shaped * adapter_hot[:, :, None], axis=1)


def expand_rank_rows(low_rows, adapter_hot):
    spread_rows = adapter_hot.astype(jnp.bfloat16)[:, :, None] * low_rows[:, None, :]
    return spread_rows.reshape(low_rows.shape[0], ADAPTER_TOTAL * ADAPTER_RANK)


def layer_rows(
    attention_rows,
    residual_rows,
    token_rank,
    request_length,
    request_group,
    adapter_per_group,
    output_weight,
    output_down_maps,
    output_up_maps,
    modulation,
    hidden_down_maps,
    hidden_up_maps,
    up_weight,
    down_weight,
):
    column_index = lax.axis_index("mlp")
    shard_hidden_width = residual_rows.shape[1]
    adapter_hot, mod_rows = token_tables(
        token_rank, request_length, request_group, adapter_per_group, modulation
    )
    shift_rows = mod_rows[:, 0]
    scale_rows = mod_rows[:, 1]
    gate_rows = lax.dynamic_slice_in_dim(
        mod_rows[:, 2], column_index * shard_hidden_width, shard_hidden_width, 1
    )
    head_terms = jnp.dot(
        attention_rows,
        lax.all_gather(output_weight, "req", axis=1, tiled=True),
        preferred_element_type=jnp.float32,
    )
    projection_rows = lax.psum_scatter(
        head_terms.astype(jnp.bfloat16), "mlp", scatter_dimension=1, tiled=True
    ).astype(jnp.float32)
    output_rank_rows = jnp.dot(
        attention_rows,
        output_down_maps.reshape(attention_rows.shape[1], ADAPTER_TOTAL * ADAPTER_RANK),
        preferred_element_type=jnp.float32,
    )
    output_rank_values = lax.psum(
        select_low(output_rank_rows, adapter_hot).astype(jnp.bfloat16), "mlp"
    )
    adapter_delta = jnp.dot(
        expand_rank_rows(output_rank_values, adapter_hot),
        output_up_maps.reshape(ADAPTER_TOTAL * ADAPTER_RANK, shard_hidden_width),
        preferred_element_type=jnp.float32,
    )
    blended_rows = (residual_rows.astype(jnp.float32) + projection_rows + adapter_delta).astype(
        jnp.bfloat16
    )
    values = blended_rows.astype(jnp.float32)
    full_rows = lax.all_gather(blended_rows, "mlp", axis=1, tiled=True).astype(jnp.float32)
    row_mean = jnp.sum(full_rows, axis=1, keepdims=True) / MODEL_WIDTH
    variance = (
        jnp.sum(full_rows * full_rows, axis=1, keepdims=True) / MODEL_WIDTH - row_mean * row_mean
    )
    normalized_rows = (
        (full_rows - row_mean) * lax.rsqrt(variance + norm_epsilon) * (1.0 + scale_rows)
        + shift_rows
    ).astype(jnp.bfloat16)
    normed_local = lax.dynamic_slice_in_dim(
        normalized_rows, column_index * shard_hidden_width, shard_hidden_width, 1
    )
    part_low = jnp.dot(
        normed_local,
        hidden_down_maps.reshape(shard_hidden_width, ADAPTER_TOTAL * ADAPTER_RANK),
        preferred_element_type=jnp.float32,
    )
    hidden_rank_values = lax.psum(select_low(part_low, adapter_hot).astype(jnp.bfloat16), "mlp")
    hidden_unit_width = up_weight.shape[1]
    hidden_total = jnp.dot(
        normalized_rows,
        lax.all_gather(up_weight, "req", axis=0, tiled=True),
        preferred_element_type=jnp.float32,
    )
    hidden_total = hidden_total + jnp.dot(
        expand_rank_rows(hidden_rank_values, adapter_hot),
        hidden_up_maps.reshape(ADAPTER_TOTAL * ADAPTER_RANK, hidden_unit_width),
        preferred_element_type=jnp.float32,
    )
    hidden = jax.nn.gelu(hidden_total, approximate=True).astype(jnp.bfloat16)
    down_terms = jnp.dot(
        hidden,
        lax.all_gather(down_weight, "req", axis=1, tiled=True),
        preferred_element_type=jnp.float32,
    )
    down_sum = lax.psum_scatter(
        down_terms.astype(jnp.bfloat16), "mlp", scatter_dimension=1, tiled=True
    ).astype(jnp.float32)
    return (values + gate_rows * down_sum).astype(jnp.bfloat16)


def local(
    residual_input,
    attention_output,
    request_length,
    request_group,
    adapter_per_group,
    output_weight,
    output_down_maps,
    output_up_maps,
    modulation,
    hidden_down_maps,
    hidden_up_maps,
    up_weight,
    down_weight,
):
    req_count = lax.axis_size("req")
    device_index = lax.axis_index("req")
    live_rows = jnp.sum(request_length, axis=1)
    dev_ends = jnp.cumsum(live_rows)
    dev_starts = dev_ends - live_rows
    offset = dev_starts[device_index]
    shard_hidden_width = residual_input.shape[1]
    weights = (
        request_length,
        request_group,
        adapter_per_group,
        output_weight,
        output_down_maps,
        output_up_maps,
        modulation,
        hidden_down_maps,
        hidden_up_maps,
        up_weight,
        down_weight,
    )
    token_rank = jnp.minimum(offset + jnp.arange(CAP, dtype=jnp.int32), TOK_DEV * req_count - 1)
    packed_out = layer_rows(attention_output, residual_input, token_rank, *weights)
    moved_out = lax.all_to_all(
        send_layout(packed_out, offset, req_count), "req", split_axis=1, concat_axis=1, tiled=True
    )
    result = compact(moved_out, dev_starts, dev_ends, req_count, device_index)
    return result.reshape(TOK_DEV, 1, shard_hidden_width)


def solution(mesh):
    placed = (
        P("req", "mlp"),
        P("req", "mlp"),
        P(),
        P(),
        P(),
        P("mlp", "req"),
        P("mlp", None, None),
        P(None, None, "mlp"),
        P(),
        P("mlp", None, None),
        P(None, None, "mlp"),
        P("req", "mlp"),
        P("mlp", "req"),
    )
    return jax.shard_map(
        local, mesh=mesh, in_specs=placed, out_specs=P(None, "req", "mlp"), check_vma=False
    )
```

profile of v0, /device:TPU:9, one launch (start us, length us, event | category | flops | bytes accessed | tf_op | source)
XLA Modules:
  0.0 418.9 jit_solution(15654548941162831555)
XLA Ops:
  6.5 0.7 all-gather.5.cloned.1.call-update
  7.3 0.0 reduce-scatter.7.cloned.1.call-start
  7.3 54.6 %all-gather.5.cloned.1.call-done = bf16[384,5120]{0,1:T(8,128)(2,1)} async-done(((bf16[384,320]{0,1:T(8,128)(2,1)}), bf16[384,5120]{0,1:T(8,128)(2,1)}) %all-gather.5.cloned.1.call-update) | async-done | bytes 3932176 | tf_op jit(solution)/shard_map/all_gather | solution.py:89
  61.9 8.1 %convolution_convert_fusion.1 = bf16[576,5120]{1,0:T(8,128)(2,1)} fusion(bf16[576,384]{1,0:T(8,128)(2,1)} %param.14, bf16[384,5120]{0,1:T(8,128)(2,1)} %all-gather.5.cloned.1.call-done), kind=kOutput, calls=%fused_computation.13 | convolution fusion | flops 2267873280 | bytes 10272768 | tf_op jit(solution)/shard_map/dot_general | solution.py:87
  70.0 8.6 %copy.34 = bf16[576,5120]{0,1:T(8,128)(2,1)} copy(bf16[576,5120]{1,0:T(8,128)(2,1)} %convolution_convert_fusion.1) | data formatting | bytes 11796480
  78.6 0.0 copy-start.13
  78.6 0.0 copy-start.8
  78.7 0.0 copy-start.11
  78.7 0.0 reduce-scatter.7.cloned.1.call-update
  78.7 0.0 all-gather.7.cloned.1.call-start
  78.7 0.6 copy-done.5
  79.3 0.1 copy.29
  79.4 0.1 copy.28
  79.5 0.1 reduce
  79.7 0.1 reshape.287
  79.7 0.1 reduce-window.16
  79.8 0.1 reduce.1
  79.9 0.6 dynamic_slice.15
  80.5 0.6 add_minimum_fusion
  81.2 0.1 convert_reduce_fusion.1
  81.3 0.1 select_reduce_fusion
  81.4 0.1 select_reduce_fusion.2
  81.5 0.4 fusion.18
  81.9 20.7 %psum.14 = bf16[576,16]{0,1:T(8,128)(2,1)S(1)} all-reduce(bf16[576,16]{0,1:T(8,128)(2,1)S(1)} %fusion.18), channel_id=1, replica_groups=mesh['req'=16,'mlp'=8] {'mlp'}, use_global_device_ids=true, to_apply=%region_10.11 | all-reduce | flops 9216 | bytes 36864 | tf_op jit(solution)/shard_map/psum | solution.py:100
  102.6 19.1 %reduce-scatter.7.cloned.1.call-done = bf16[640,576]{1,0:T(8,128)(2,1)} async-done(((bf16[5120,576]{1,0:T(8,128)(2,1)}), bf16[640,576]{1,0:T(8,128)(2,1)}) %reduce-scatter.7.cloned.1.call-update) | async-done | bytes 737296
  121.8 1.5 copy.35
  123.3 0.0 copy-done.11
  123.3 1.3 fusion.16
  124.6 0.0 all-gather.7.cloned.1.call-update
  124.6 0.0 all-gather.9.cloned.1.call-start
  124.6 0.5 all-gather.9.cloned.1.call-update
  125.2 0.0 all-gather.11.cloned.1.call-start
  125.2 0.5 all-gather.11.cloned.1.call-update
  125.8 0.2 reduce-scatter.9.cloned.1.call-start
  126.0 18.4 %fusion.22 = f32[576,3,5120]{2,0,1:T(8,128)} fusion(f32[8,3,5120]{2,0,1:T(8,128)S(1)} %copy-done, s32[576]{0:T(1024)S(1)} %select_reduce_fusion), kind=kOutput, calls=%fused_computation.38 | convolution fusion | flops 849351168 | bytes 35883264 | tf_op jit(solution)/shard_map/dot_general | solution.py:43
  144.4 19.8 %all-gather.7.cloned.1.call-done = bf16[576,5120]{1,0:T(8,128)(2,1)} async-done(((bf16[576,640]{1,0:T(8,128)(2,1)}), bf16[576,5120]{1,0:T(8,128)(2,1)}) %all-gather.7.cloned.1.call-update) | async-done | bytes 5898256 | tf_op jit(solution)/shard_map/all_gather | solution.py:112
  164.2 4.6 %convert_reduce_fusion = (f32[576]{0:T(1024)S(1)}, f32[576]{0:T(1024)S(1)}) fusion(bf16[576,5120]{1,0:T(8,128)(2,1)} %all-gather.7.cloned.1.call-done), kind=kLoop, calls=%fused_computation.3 | loop fusion | flops 11795328 | bytes 5902848 | tf_op jit(solution)/shard_map/reduce_sum | solution.py:113
  168.8 0.0 copy-done.2
  168.8 0.0 copy-start.12
  168.8 9.6 %fusion.3 = bf16[576,5120]{1,0:T(8,128)(2,1)S(1)} fusion(bf16[576,5120]{1,0:T(8,128)(2,1)S(1)} %copy-done.2, f32[576,3,5120]{2,0,1:T(8,128)} %fusion.22, f32[576]{0:T(1024)S(1)} %get-tuple-element.8, f32[576]{0:T(1024)S(1)} %get-tuple-element.7), kind=kLoop, calls=%fused_computation.7 | loop fusion | flops 20643840 | bytes 35394048 | tf_op jit(solution)/shard_map/convert_element_type | solution.py:120
  178.5 2.5 copy-done.3
  181.0 0.5 fusion.17
  181.4 20.5 %psum.15 = bf16[576,16]{0,1:T(8,128)(2,1)S(1)} all-reduce(bf16[576,16]{0,1:T(8,128)(2,1)S(1)} %fusion.17), channel_id=1, replica_groups=mesh['req'=16,'mlp'=8] {'mlp'}, use_global_device_ids=true, to_apply=%region_14.15 | all-reduce | flops 9216 | bytes 36864 | tf_op jit(solution)/shard_map/psum | solution.py:129
  202.0 39.1 %all-gather.9.cloned.1.call-done = bf16[5120,864]{1,0:T(8,128)(2,1)} async-done(((bf16[320,864]{1,0:T(8,128)(2,1)}), bf16[5120,864]{1,0:T(8,128)(2,1)}) %all-gather.9.cloned.1.call-update) | async-done | bytes 8847376 | tf_op jit(solution)/shard_map/all_gather | solution.py:133
  241.1 11.9 %fusion.44 = f32[576,864]{1,0:T(8,128)} fusion(bf16[576,5120]{1,0:T(8,128)(2,1)} %copy-done.3, bf16[5120,864]{1,0:T(8,128)(2,1)} %all-gather.9.cloned.1.call-done), kind=kOutput, calls=%fused_computation.87 | convolution fusion | flops 5096079360 | bytes 16736256 | tf_op jit(solution)/shard_map/dot_general | solution.py:131
  253.0 64.2 %all-gather.11.cloned.1.call-done = bf16[864,5120]{0,1:T(8,128)(2,1)} async-done(((bf16[864,320]{0,1:T(8,128)(2,1)}), bf16[864,5120]{0,1:T(8,128)(2,1)}) %all-gather.11.cloned.1.call-update) | async-done | bytes 8847376 | tf_op jit(solution)/shard_map/all_gather | solution.py:144
  317.2 0.0 copy-done.9
  317.2 12.2 %convolution_convert_fusion = bf16[576,5120]{1,0:T(8,128)(2,1)} fusion(bf16[864,5120]{0,1:T(8,128)(2,1)} %all-gather.11.cloned.1.call-done, f32[576,864]{1,0:T(8,128)} %fusion.44, bf16[16,16,864]{2,1,0:T(8,128)(2,1)S(1)} %copy-done.9, bf16[576,16]{0,1:T(8,128)(2,1)S(1)} %psum.15, bf16[576,16]{0,1:T(8,128)(2,1)S(1)} %get-tuple-element.9), kind=kOutput, calls=%fused_computation.12 | convolution fusion | flops 5358956544 | bytes 17215488 | tf_op jit(solution)/shard_map/dot_general | solution.py:142
  329.4 8.6 %copy.36 = bf16[576,5120]{0,1:T(8,128)(2,1)} copy(bf16[576,5120]{1,0:T(8,128)(2,1)} %convolution_convert_fusion) | data formatting | bytes 11796480
  338.0 0.0 reduce-scatter.9.cloned.1.call-update
  338.0 10.4 %slice.14 = f32[576,1,5120]{2,0,1:T(8,128)} slice(f32[576,3,5120]{2,0,1:T(8,128)} %fusion.22), slice={[0:576], [2:3], [0:5120]} | slice | bytes 23592960 | tf_op jit(solution)/shard_map/slice | solution.py:85
  350.3 30.5 %reduce-scatter.9.cloned.1.call-done = bf16[640,576]{1,0:T(8,128)(2,1)} async-done(((bf16[5120,576]{1,0:T(8,128)(2,1)}), bf16[640,576]{1,0:T(8,128)(2,1)}) %reduce-scatter.9.cloned.1.call-update) | async-done | bytes 737296
  380.8 1.5 copy.37
  382.3 1.6 fusion.15
  383.9 0.0 copy-start.1
  383.9 0.1 copy.31
  384.1 1.3 fusion.19
  385.3 6.7 %all-to-all-start = ((bf16[36,16,640]{2,0,1:T(8,128)(2,1)}), bf16[36,16,640]{2,0,1:T(8,128)(2,1)S(1)}, u32[]{:S(2)}, u32[]{:S(2)}) async-start(bf16[36,16,640]{2,0,1:T(8,128)(2,1)} %fusion.19), calls=%async_computation | async-start | bytes 1638400 | tf_op jit(solution)/shard_map/all_to_all | solution.py:190
  392.0 0.1 convert_reduce_fusion.2
  392.1 0.1 select_reduce_fusion.1
  392.3 16.5 %all-to-all-done = bf16[36,16,640]{2,0,1:T(8,128)(2,1)S(1)} async-done(((bf16[36,16,640]{2,0,1:T(8,128)(2,1)}), bf16[36,16,640]{2,0,1:T(8,128)(2,1)S(1)}, u32[]{:S(2)}, u32[]{:S(2)}) %all-to-all-start) | async-done | bytes 737312 | tf_op jit(solution)/shard_map/all_to_all | solution.py:190
  408.8 0.1 copy.33
  408.9 2.2 gather_fusion
  411.1 0.9 bitcast_select_fusion
  (29 shorter events, 0.2 us)
Async XLA Ops:
  6.5 119.5 %copy-start = (f32[8,3,5120]{2,0,1:T(8,128)S(1)}, f32[8,3,5120]{2,0,1:T(8,128)}, u32[]{:S(2)}) copy-start(f32[8,3,5120]{2,0,1:T(8,128)} %param.21) | copy-start | bytes 1474564
  6.5 55.4 %all-gather.5.cloned.1.call-start = ((), (), s32[]{:S(2)}) async-start(), calls=%async_computation.3 | async-start | bytes 4177920 | tf_op jit(solution)/shard_map/all_gather | solution.py:89
  7.3 114.5 %reduce-scatter.7.cloned.1.call-start = ((), (), s32[]{:S(2)}) async-start(), calls=%async_computation.7 | async-start | bytes 7372800
  78.6 0.7 copy-start.5
  78.6 2.7 copy-start.6
  78.6 2.8 copy-start.7
  78.6 2.9 copy-start.10
  78.6 2.9 copy-start.13
  78.6 44.6 %copy-start.8 = (bf16[576,640]{1,0:T(8,128)(2,1)S(1)}, bf16[576,640]{1,0:T(8,128)(2,1)}, u32[]{:S(2)}) copy-start(bf16[576,640]{1,0:T(8,128)(2,1)} %param.13) | copy-start | bytes 2211844
  78.7 44.6 %copy-start.11 = (bf16[16,16,640]{2,1,0:T(8,128)(2,1)S(1)}, bf16[16,16,640]{2,1,0:T(8,128)(2,1)}, u32[]{:S(2)}) copy-start(bf16[16,16,640]{2,1,0:T(8,128)(2,1)} %param.20) | copy-start | bytes 983044
  78.7 85.5 %all-gather.7.cloned.1.call-start = ((), (), s32[]{:S(2)}) async-start(), calls=%async_computation.4 | async-start | bytes 6635520 | tf_op jit(solution)/shard_map/all_gather | solution.py:112
  124.6 116.5 %all-gather.9.cloned.1.call-start = ((), (), s32[]{:S(2)}) async-start(), calls=%async_computation.5 | async-start | bytes 9748480 | tf_op jit(solution)/shard_map/all_gather | solution.py:133
  125.2 192.0 %all-gather.11.cloned.1.call-start = ((), (), s32[]{:S(2)}) async-start(), calls=%async_computation.6 | async-start | bytes 9748480 | tf_op jit(solution)/shard_map/all_gather | solution.py:144
  125.8 255.0 %reduce-scatter.9.cloned.1.call-start = ((), (), s32[]{:S(2)}) async-start(), calls=%async_computation.8 | async-start | bytes 7372800
  164.2 4.6 %copy-start.2 = (bf16[576,5120]{1,0:T(8,128)(2,1)S(1)}, bf16[576,5120]{1,0:T(8,128)(2,1)}, u32[]{:S(2)}) copy-start(bf16[576,5120]{1,0:T(8,128)(2,1)} %all-gather.7.cloned.1.call-done) | copy-start | bytes 17694724
  168.8 12.1 %copy-start.12 = (bf16[640,16,16]{0,2,1:T(8,128)(2,1)S(1)}, bf16[640,16,16]{0,2,1:T(8,128)(2,1)}, u32[]{:S(2)}) copy-start(bf16[640,16,16]{0,2,1:T(8,128)(2,1)} %param.22) | copy-start | bytes 983044
  178.5 2.5 copy-start.3
  202.0 115.2 %copy-start.9 = (bf16[16,16,864]{2,1,0:T(8,128)(2,1)S(1)}, bf16[16,16,864]{2,1,0:T(8,128)(2,1)}, u32[]{:S(2)}) copy-start(bf16[16,16,864]{2,1,0:T(8,128)(2,1)} %param.23) | copy-start | bytes 1327108
  338.0 44.3 %copy-start.4 = (bf16[576,640]{1,0:T(8,128)(2,1)S(1)}, bf16[576,640]{1,0:T(8,128)(2,1)}, u32[]{:S(2)}) copy-start(bf16[576,640]{1,0:T(8,128)(2,1)} %fusion.16) | copy-start | bytes 2211844
  383.9 28.1 %copy-start.1 = (f32[8,3,5120]{2,0,1:T(8,128)S(1)}, f32[8,3,5120]{2,0,1:T(8,128)}, u32[]{:S(2)}) copy-start(f32[8,3,5120]{2,0,1:T(8,128)} %param.21) | copy-start | bytes 1474564
  385.3 23.5 %all-to-all-start = ((bf16[36,16,640]{2,0,1:T(8,128)(2,1)}), bf16[36,16,640]{2,0,1:T(8,128)(2,1)S(1)}, u32[]{:S(2)}, u32[]{:S(2)}) async-start(bf16[36,16,640]{2,0,1:T(8,128)(2,1)} %fusion.19), calls=%async_computation | async-start | bytes 1638400 | tf_op jit(solution)/shard_map/all_to_all | solution.py:190
Sparse Core Ops, SparseCore 0:
  9.5 52.4 all-gather.4
  78.8 42.9 reduce-scatter.6
  124.7 39.4 all-gather.6
  166.2 74.9 all-gather.8
  243.1 74.0 all-gather.10
  338.1 42.6 reduce-scatter.8
where the time goes:
time: 420 us; the launch traced here: 419 us
  waiting for transfers between devices  246 us (59%)
  matrix products  52.6 us (13%)
  blocking collectives  41.2 us (10%)
  local copies, waits for them, and re-layouts  37 us (9%)
  other arithmetic  19.6 us (5%)
  between operations  15.7 us (4%)
  starting transfers between devices  7.06 us (2%)
    all_gather x1, waiting for transfers between devices, layer_rows(): lax.all_gather(down_weight, 'req', axis=1, tiled=True)  64.2 us
    all_gather x1, waiting for transfers between devices, layer_rows(): lax.all_gather(output_weight, 'req', axis=1, tiled=True)  54.6 us
    unnamed x8, waiting for transfers between devices  51.4 us
    all_gather x1, waiting for transfers between devices, layer_rows(): lax.all_gather(up_weight, 'req', axis=0, tiled=True)  39.1 us
    unnamed x33, local copies, waits for them, and re-layouts  23.4 us
    psum x1, blocking collectives, layer_rows(): lax.psum(select_low(output_rank_rows, adapter_hot).astype(jnp.bfloat16),...  20.7 us
    psum x1, blocking collectives, layer_rows(): lax.psum(select_low(part_low, adapter_hot).astype(jnp.bfloat16), 'mlp')  20.5 us
    all_gather x1, waiting for transfers between devices, layer_rows(): lax.all_gather(blended_rows, 'mlp', axis=1, tiled=True).astype(jnp.float32)  19.8 us
  transfers between devices with their start and end apart: 7, of which 7 were waited for; matrix products, arithmetic and copies ran while one was open for 14% of the time, Pallas kernels for 0%

commit v1 on v0

--- a/solution.py
+++ b/solution.py
@@ -1,3 +1,4 @@
+import functools
 import jax
 import jax.numpy as jnp
 from jax import lax
@@ -9,6 +10,37 @@
 TOK_DEV = 384
 CAP = 576
 norm_epsilon = 1e-06
+
+
+def supply_all_steps_all(xin, mesh_dim):
+    aux, local_now, state_next = (lax.axis_size(mesh_dim), lax.axis_index(mesh_dim), xin.shape[1])
+    q_next = lax.dynamic_update_slice_in_dim(
+        jnp.zeros([c * aux if at == 1 else c for at, c in enumerate(xin.shape)], xin.dtype),
+        xin,
+        local_now * state_next,
+        axis=1,
+    )
+    z_new = response = xin
+    dev_j = 1
+    while dev_j < aux // 2 + 1:
+        z_new = lax.ppermute(
+            z_new, axis_name=mesh_dim, perm=[(at, (at + 1) % aux) for at in range(aux)]
+        )
+        q_next = lax.dynamic_update_slice_in_dim(
+            q_next, z_new, (local_now - dev_j) % aux * state_next, axis=1
+        )
+        if 2 * dev_j < aux:
+            response = lax.ppermute(
+                response, axis_name=mesh_dim, perm=[(at, (at - 1) % aux) for at in range(aux)]
+            )
+            q_next = lax.dynamic_update_slice_in_dim(
+                q_next, response, (local_now + dev_j) % aux * state_next, axis=1
+            )
+        dev_j = dev_j + 1
+    return q_next
+
+
+try_all_core = functools.partial(supply_all_steps_all, mesh_dim="mlp")
 
 
 def send_layout(packed, offset, req_count):
@@ -109,7 +141,7 @@
         jnp.bfloat16
     )
     values = blended_rows.astype(jnp.float32)
-    full_rows = lax.all_gather(blended_rows, "mlp", axis=1, tiled=True).astype(jnp.float32)
+    full_rows = try_all_core(blended_rows).astype(jnp.float32)
     row_mean = jnp.sum(full_rows, axis=1, keepdims=True) / MODEL_WIDTH
     variance = (
         jnp.sum(full_rows * full_rows, axis=1, keepdims=True) / MODEL_WIDTH - row_mean * row_mean

time: 420 us -> 376 us (0.90)
  waiting for transfers between devices: 246 us -> 176 us
  local copies, waits for them, and re-layouts: 37 us -> 49 us
  starting transfers between devices: 7.06 us -> 14.2 us
  blocking collectives: 41.2 us -> 47.5 us
    all_gather x1, waiting for transfers between devices: 39.1 us -> 0.02 us  [layer_rows(): lax.all_gather(up_weight, 'req', axis=0, tiled=True)]
    all_gather x1, waiting for transfers between devices: 64.2 us -> 36.4 us  [layer_rows(): lax.all_gather(down_weight, 'req', axis=1, tiled=True)]
    all_gather x1 -> x0, waiting for transfers between devices: 19.8 us -> none  [layer_rows(): lax.all_gather(blended_rows, 'mlp', axis=1, tiled=True).astype(jnp.float32)]
    ppermute x0 -> x7, waiting for transfers between devices: none -> 17.7 us  [the longest x4 16.6 us: supply_all_steps_all(): lax.ppermute(z_new, axis_name=mesh_dim, perm=[(at, (at + 1) % aux) for at...]
    dynamic_update_slice x0 -> x7, local copies, waits for them, and re-layouts: none -> 9.22 us  [the longest x4 5.13 us: supply_all_steps_all(): lax.dynamic_update_slice_in_dim(q_next, z_new, (local_now - dev_j) % aux...]
    ppermute x0 -> x7, starting transfers between devices: none -> 7.36 us  [the longest x4 7.35 us: supply_all_steps_all(): lax.ppermute(z_new, axis_name=mesh_dim, perm=[(at, (at + 1) % aux) for at...]
    psum x1, blocking collectives: 20.5 us -> 26.8 us  [layer_rows(): lax.psum(select_low(part_low, adapter_hot).astype(jnp.bfloat16), 'mlp')]
    unnamed x8 -> x7, waiting for transfers between devices: 51.4 us -> 50.7 us
  transfers between devices with their start and end apart: 7 -> 13, of which waited for: 7 -> 10; matrix products, arithmetic and copies ran while one was open for 14% -> 20% of each run, Pallas kernels for 0% -> 0%
where the time goes in v1:
time: 376 us; the launch traced here: 375 us
  waiting for transfers between devices  176 us (47%)
  matrix products  51.8 us (14%)
  local copies, waits for them, and re-layouts  49 us (13%)
  blocking collectives  47.5 us (13%)
  other arithmetic  21.4 us (6%)
  between operations  15.4 us (4%)
  starting transfers between devices  14.2 us (4%)
    all_gather x1, waiting for transfers between devices, layer_rows(): lax.all_gather(output_weight, 'req', axis=1, tiled=True)  54.6 us
    unnamed x7, waiting for transfers between devices  50.7 us
    all_gather x1, waiting for transfers between devices, layer_rows(): lax.all_gather(down_weight, 'req', axis=1, tiled=True)  36.4 us
    psum x1, blocking collectives, layer_rows(): lax.psum(select_low(part_low, adapter_hot).astype(jnp.bfloat16), 'mlp')  26.8 us
    unnamed x33, local copies, waits for them, and re-layouts  23 us
    psum x1, blocking collectives, layer_rows(): lax.psum(select_low(output_rank_rows, adapter_hot).astype(jnp.bfloat16),...  20.7 us
    dot_general x1, matrix products, token_tables(): jnp.dot(group_hot.astype(jnp.float32), modulation.reshape(group_count, -1...  18.2 us
    ppermute x4, waiting for transfers between devices, supply_all_steps_all(): lax.ppermute(z_new, axis_name=mesh_dim, perm=[(at, (at + 1) % aux) for at...  16.6 us
  transfers between devices with their start and end apart: 13, of which 10 were waited for; matrix products, arithmetic and copies ran while one was open for 20% of the time, Pallas kernels for 0%

profile of v1, /device:TPU:9, one launch (start us, length us, event | category | flops | bytes accessed | tf_op | source)
XLA Modules:
  0.0 375.0 jit_solution(7013035820116279319)
XLA Ops:
  6.5 0.7 all-gather.4.cloned.1.call-update
  7.3 54.6 %all-gather.4.cloned.1.call-done = bf16[384,5120]{0,1:T(8,128)(2,1)} async-done(((bf16[384,320]{0,1:T(8,128)(2,1)}), bf16[384,5120]{0,1:T(8,128)(2,1)}) %all-gather.4.cloned.1.call-update) | async-done | bytes 3932176 | tf_op jit(solution)/shard_map/all_gather | solution.py:121
  61.9 8.0 %convolution_convert_fusion.1 = bf16[576,5120]{1,0:T(8,128)(2,1)} fusion(bf16[576,384]{1,0:T(8,128)(2,1)} %param.14, bf16[384,5120]{0,1:T(8,128)(2,1)} %all-gather.4.cloned.1.call-done), kind=kOutput, calls=%fused_computation.13 | convolution fusion | flops 2267873280 | bytes 10272768 | tf_op jit(solution)/shard_map/dot_general | solution.py:119
  69.9 8.8 %copy.34 = bf16[576,5120]{0,1:T(8,128)(2,1)} copy(bf16[576,5120]{1,0:T(8,128)(2,1)} %convolution_convert_fusion.1) | data formatting | bytes 11796480
  78.8 0.0 all-gather.6.cloned.1.call-start
  78.8 0.7 all-gather.6.cloned.1.call-update
  79.6 0.5 all-gather.8.cloned.1.call-update
  80.2 0.1 copy.29
  80.3 0.1 copy.28
  80.4 0.1 reduce
  80.5 0.1 reshape.287
  80.6 0.1 reduce-window.16
  80.7 0.1 reduce.1
  80.8 0.6 dynamic_slice.15
  81.4 0.6 add_minimum_fusion
  82.0 0.1 convert_reduce_fusion.1
  82.2 0.1 select_reduce_fusion
  82.3 0.1 select_reduce_fusion.2
  82.4 0.4 fusion.18
  82.8 20.7 %psum.14 = bf16[576,16]{0,1:T(8,128)(2,1)S(1)} all-reduce(bf16[576,16]{0,1:T(8,128)(2,1)S(1)} %fusion.18), channel_id=1, replica_groups=mesh['req'=16,'mlp'=8] {'mlp'}, use_global_device_ids=true, to_apply=%region_10.11 | all-reduce | flops 9216 | bytes 36864 | tf_op jit(solution)/shard_map/psum | solution.py:132
  103.5 18.3 %reduce-scatter.7.cloned.1.call-done = bf16[640,576]{1,0:T(8,128)(2,1)} async-done(((bf16[5120,576]{1,0:T(8,128)(2,1)}), bf16[640,576]{1,0:T(8,128)(2,1)}) %reduce-scatter.7.cloned.1.call-update) | async-done | bytes 737296
  121.8 1.5 copy.35
  123.3 3.2 broadcast_in_dim.79
  126.5 1.4 constant_dynamic-update-slice_fusion.7
  127.9 0.6 collective-permute-start
  128.5 8.4 %collective-permute-done = bf16[576,640]{1,0:T(8,128)(2,1)S(1)} collective-permute-done((bf16[576,640]{1,0:T(8,128)(2,1)S(1)}, bf16[576,640]{1,0:T(8,128)(2,1)S(1)}, u32[]{:S(2)}, u32[]{:S(2)}) %collective-permute-start) | collective-permute-done | bytes 737312 | tf_op jit(solution)/shard_map/ppermute | solution.py:26
  136.9 2.5 collective-permute-start.2
  139.4 0.4 collective-permute-done.1
  139.8 8.0 %collective-permute-done.2 = bf16[576,640]{1,0:T(8,128)(2,1)} collective-permute-done((bf16[576,640]{1,0:T(8,128)(2,1)S(1)}, bf16[576,640]{1,0:T(8,128)(2,1)}, u32[]{:S(2)}, u32[]{:S(2)}) %collective-permute-start.2) | collective-permute-done | bytes 737312 | tf_op jit(solution)/shard_map/ppermute | solution.py:26
  147.8 2.6 collective-permute-start.4
  150.3 0.7 collective-permute-done.3
  151.1 18.2 %fusion.22 = f32[576,3,5120]{2,0,1:T(8,128)} fusion(f32[8,3,5120]{2,0,1:T(8,128)S(1)} %copy-done, s32[576]{0:T(1024)S(1)} %select_reduce_fusion), kind=kOutput, calls=%fused_computation.38 | convolution fusion | flops 849351168 | bytes 35883264 | tf_op jit(solution)/shard_map/dot_general | solution.py:75
  169.2 1.7 collective-permute-start.6
  171.0 1.0 constant_dynamic-update-slice_fusion.6
  172.0 1.0 constant_dynamic-update-slice_fusion.5
  173.0 2.1 constant_dynamic-update-slice_fusion.4
  175.1 1.0 constant_dynamic-update-slice_fusion.3
  176.1 1.0 constant_dynamic-update-slice_fusion.2
  177.1 2.1 constant_dynamic-update-slice_fusion.1
  179.2 0.2 collective-permute-done.6
  179.4 1.0 constant_dynamic-update-slice_fusion
  180.3 4.7 %convert_reduce_fusion = (f32[576]{0:T(1024)S(1)}, f32[576]{0:T(1024)S(1)}) fusion(bf16[576,5120]{1,0:T(8,128)(2,1)} %constant_dynamic-update-slice_fusion), kind=kLoop, calls=%fused_computation.3 | loop fusion | flops 11795328 | bytes 5902848 | tf_op jit(solution)/shard_map/reduce_sum | solution.py:145
  185.0 11.4 %fusion.3 = bf16[576,5120]{1,0:T(8,128)(2,1)S(1)} fusion(bf16[576,5120]{1,0:T(8,128)(2,1)} %constant_dynamic-update-slice_fusion, f32[576,3,5120]{2,0,1:T(8,128)} %fusion.22, f32[576]{0:T(1024)S(1)} %get-tuple-element.8, f32[576]{0:T(1024)S(1)} %get-tuple-element.7), kind=kLoop, calls=%fused_computation.7 | loop fusion | flops 20643840 | bytes 35394048 | tf_op jit(solution)/shard_map/convert_element_type | solution.py:152
  196.4 2.5 copy-done.2
  198.9 0.5 fusion.17
  199.4 26.8 %psum.15 = bf16[576,16]{0,1:T(8,128)(2,1)S(1)} all-reduce(bf16[576,16]{0,1:T(8,128)(2,1)S(1)} %fusion.17), channel_id=1, replica_groups=mesh['req'=16,'mlp'=8] {'mlp'}, use_global_device_ids=true, to_apply=%region_14.15 | all-reduce | flops 9216 | bytes 36864 | tf_op jit(solution)/shard_map/psum | solution.py:161
  226.2 0.5 fusion.26
  226.7 12.1 %fusion.13 = bf16[576,864]{1,0:T(8,128)(2,1)} fusion(f32[576,864,1]{1,0,2:T(8,128)S(1)} %fusion.26, bf16[576,5120]{1,0:T(8,128)(2,1)} %copy-done.2, bf16[5120,864]{1,0:T(8,128)(2,1)} %all-gather.6.cloned.1.call-done), kind=kOutput, calls=%fused_computation.22 | convolution fusion | flops 5101056000 | bytes 17731584 | tf_op jit(solution)/shard_map/dot_general | solution.py:163
  238.8 36.4 %all-gather.8.cloned.1.call-done = bf16[864,5120]{0,1:T(8,128)(2,1)} async-done(((bf16[864,320]{0,1:T(8,128)(2,1)}), bf16[864,5120]{0,1:T(8,128)(2,1)}) %all-gather.8.cloned.1.call-update) | async-done | bytes 8847376 | tf_op jit(solution)/shard_map/all_gather | solution.py:176
  275.2 10.7 %convolution_convert_fusion = bf16[576,5120]{1,0:T(8,128)(2,1)} fusion(bf16[576,864]{1,0:T(8,128)(2,1)} %fusion.13, bf16[864,5120]{0,1:T(8,128)(2,1)} %all-gather.8.cloned.1.call-done), kind=kOutput, calls=%fused_computation.12 | convolution fusion | flops 5099028480 | bytes 15740928 | tf_op jit(solution)/shard_map/dot_general | solution.py:174
  285.9 8.6 %copy.36 = bf16[576,5120]{0,1:T(8,128)(2,1)} copy(bf16[576,5120]{1,0:T(8,128)(2,1)} %convolution_convert_fusion) | data formatting | bytes 11796480
  294.5 10.4 %slice.14 = f32[576,1,5120]{2,0,1:T(8,128)} slice(f32[576,3,5120]{2,0,1:T(8,128)} %fusion.22), slice={[0:576], [2:3], [0:5120]} | slice | bytes 23592960 | tf_op jit(solution)/shard_map/slice | solution.py:117
  306.8 30.5 %reduce-scatter.9.cloned.1.call-done = bf16[640,576]{1,0:T(8,128)(2,1)} async-done(((bf16[5120,576]{1,0:T(8,128)(2,1)}), bf16[640,576]{1,0:T(8,128)(2,1)}) %reduce-scatter.9.cloned.1.call-update) | async-done | bytes 737296
  337.3 1.5 copy.37
  338.8 1.6 fusion.15
  340.4 0.1 copy.31
  340.6 1.3 fusion.19
  341.8 6.7 %all-to-all-start = ((bf16[36,16,640]{2,0,1:T(8,128)(2,1)}), bf16[36,16,640]{2,0,1:T(8,128)(2,1)S(1)}, u32[]{:S(2)}, u32[]{:S(2)}) async-start(bf16[36,16,640]{2,0,1:T(8,128)(2,1)} %fusion.19), calls=%async_computation | async-start | bytes 1638400 | tf_op jit(solution)/shard_map/all_to_all | solution.py:222
  348.5 0.1 convert_reduce_fusion.2
  348.6 0.1 select_reduce_fusion.1
  348.8 16.5 %all-to-all-done = bf16[36,16,640]{2,0,1:T(8,128)(2,1)S(1)} async-done(((bf16[36,16,640]{2,0,1:T(8,128)(2,1)}), bf16[36,16,640]{2,0,1:T(8,128)(2,1)S(1)}, u32[]{:S(2)}, u32[]{:S(2)}) %all-to-all-start) | async-done | bytes 737312 | tf_op jit(solution)/shard_map/all_to_all | solution.py:222
  365.2 0.1 copy.33
  365.3 2.2 gather_fusion
  367.5 0.9 bitcast_select_fusion
  (49 shorter events, 0.4 us)
Async XLA Ops:
  6.5 144.5 %copy-start = (f32[8,3,5120]{2,0,1:T(8,128)S(1)}, f32[8,3,5120]{2,0,1:T(8,128)}, u32[]{:S(2)}) copy-start(f32[8,3,5120]{2,0,1:T(8,128)} %param.21) | copy-start | bytes 1474564
  6.5 55.4 %all-gather.4.cloned.1.call-start = ((), (), s32[]{:S(2)}) async-start(), calls=%async_computation.3 | async-start | bytes 4177920 | tf_op jit(solution)/shard_map/all_gather | solution.py:121
  7.3 114.5 %reduce-scatter.7.cloned.1.call-start = ((), (), s32[]{:S(2)}) async-start(), calls=%async_computation.6 | async-start | bytes 7372800
  78.7 1.4 copy-start.5
  78.7 3.4 copy-start.6
  78.7 3.6 copy-start.7
  78.7 3.7 copy-start.10
  78.7 3.7 copy-start.13
  78.8 47.7 %copy-start.8 = (bf16[576,640]{1,0:T(8,128)(2,1)S(1)}, bf16[576,640]{1,0:T(8,128)(2,1)}, u32[]{:S(2)}) copy-start(bf16[576,640]{1,0:T(8,128)(2,1)} %param.13) | copy-start | bytes 2211844
  78.8 47.7 %copy-start.11 = (bf16[16,16,640]{2,1,0:T(8,128)(2,1)S(1)}, bf16[16,16,640]{2,1,0:T(8,128)(2,1)}, u32[]{:S(2)}) copy-start(bf16[16,16,640]{2,1,0:T(8,128)(2,1)} %param.20) | copy-start | bytes 983044
  78.8 147.9 %all-gather.6.cloned.1.call-start = ((), (), s32[]{:S(2)}) async-start(), calls=%async_computation.4 | async-start | bytes 9748480 | tf_op jit(solution)/shard_map/all_gather | solution.py:165
  79.5 195.6 %all-gather.8.cloned.1.call-start = ((), (), s32[]{:S(2)}) async-start(), calls=%async_computation.5 | async-start | bytes 9748480 | tf_op jit(solution)/shard_map/all_gather | solution.py:176
  80.1 257.2 %reduce-scatter.9.cloned.1.call-start = ((), (), s32[]{:S(2)}) async-start(), calls=%async_computation.7 | async-start | bytes 7372800
  127.9 23.1 %copy-start.3 = (bf16[576,640]{1,0:T(8,128)(2,1)}, bf16[576,640]{1,0:T(8,128)(2,1)S(1)}, u32[]{:S(2)}) copy-start(bf16[576,640]{1,0:T(8,128)(2,1)S(1)} %get-tuple-element.12) | copy-start | bytes 2211844
  127.9 9.0 %collective-permute-start = (bf16[576,640]{1,0:T(8,128)(2,1)S(1)}, bf16[576,640]{1,0:T(8,128)(2,1)S(1)}, u32[]{:S(2)}, u32[]{:S(2)}) collective-permute-start(bf16[576,640]{1,0:T(8,128)(2,1)S(1)} %get-tuple-element.12), channel_id=1, source_target_pairs={{0,1},{1,2},{2,3},{3,4},{4,5},{5,6},{6,7},{7,0},{8,9},{9,10},{10,1... | collective-permute-start | bytes 2211848 | tf_op jit(solution)/shard_map/ppermute | solution.py:26
  128.5 11.3 %collective-permute-start.1 = (bf16[576,640]{1,0:T(8,128)(2,1)S(1)}, bf16[576,640]{1,0:T(8,128)(2,1)S(1)}, u32[]{:S(2)}, u32[]{:S(2)}) collective-permute-start(bf16[576,640]{1,0:T(8,128)(2,1)S(1)} %get-tuple-element.12), channel_id=1, source_target_pairs={{0,7},{1,0},{2,1},{3,2},{4,3},{5,4},{6,5},{7,6},{8,15},{9,8},{10,9... | collective-permute-start | bytes 2211848 | tf_op jit(solution)/shard_map/ppermute | solution.py:33
  136.9 10.9 %collective-permute-start.2 = (bf16[576,640]{1,0:T(8,128)(2,1)S(1)}, bf16[576,640]{1,0:T(8,128)(2,1)}, u32[]{:S(2)}, u32[]{:S(2)}) collective-permute-start(bf16[576,640]{1,0:T(8,128)(2,1)S(1)} %collective-permute-done), channel_id=1, source_target_pairs={{0,1},{1,2},{2,3},{3,4},{4,5},{5,6},{6,7},{7,0},{8,9},{9,10},{10,1... | collective-permute-start | bytes 2211848 | tf_op jit(solution)/shard_map/ppermute | solution.py:26
  139.8 11.3 %collective-permute-start.3 = (bf16[576,640]{1,0:T(8,128)(2,1)S(1)}, bf16[576,640]{1,0:T(8,128)(2,1)S(1)}, u32[]{:S(2)}, u32[]{:S(2)}) collective-permute-start(bf16[576,640]{1,0:T(8,128)(2,1)S(1)} %collective-permute-done.1), channel_id=1, source_target_pairs={{0,7},{1,0},{2,1},{3,2},{4,3},{5,4},{6,5},{7,6},{8,15},{9,8},{10,9... | collective-permute-start | bytes 2211848 | tf_op jit(solution)/shard_map/ppermute | solution.py:33
  147.8 21.5 %collective-permute-start.4 = (bf16[576,640]{1,0:T(8,128)(2,1)}, bf16[576,640]{1,0:T(8,128)(2,1)S(1)}, u32[]{:S(2)}, u32[]{:S(2)}) collective-permute-start(bf16[576,640]{1,0:T(8,128)(2,1)} %collective-permute-done.2), channel_id=1, source_target_pairs={{0,1},{1,2},{2,3},{3,4},{4,5},{5,6},{6,7},{7,0},{8,9},{9,10},{10,1... | collective-permute-start | bytes 2211848 | tf_op jit(solution)/shard_map/ppermute | solution.py:26
  151.0 26.1 %collective-permute-start.5 = (bf16[576,640]{1,0:T(8,128)(2,1)S(1)}, bf16[576,640]{1,0:T(8,128)(2,1)}, u32[]{:S(2)}, u32[]{:S(2)}) collective-permute-start(bf16[576,640]{1,0:T(8,128)(2,1)S(1)} %collective-permute-done.3), channel_id=1, source_target_pairs={{0,7},{1,0},{2,1},{3,2},{4,3},{5,4},{6,5},{7,6},{8,15},{9,8},{10,9... | collective-permute-start | bytes 2211848 | tf_op jit(solution)/shard_map/ppermute | solution.py:33
  169.2 10.1 %collective-permute-start.6 = (bf16[576,640]{1,0:T(8,128)(2,1)S(1)}, bf16[576,640]{1,0:T(8,128)(2,1)S(1)}, u32[]{:S(2)}, u32[]{:S(2)}) collective-permute-start(bf16[576,640]{1,0:T(8,128)(2,1)S(1)} %collective-permute-done.4), channel_id=1, source_target_pairs={{0,1},{1,2},{2,3},{3,4},{4,5},{5,6},{6,7},{7,0},{8,9},{9,10},{10,1... | collective-permute-start | bytes 2211848 | tf_op jit(solution)/shard_map/ppermute | solution.py:26
  185.0 13.9 %copy-start.12 = (bf16[640,16,16]{0,2,1:T(8,128)(2,1)S(1)}, bf16[640,16,16]{0,2,1:T(8,128)(2,1)}, u32[]{:S(2)}) copy-start(bf16[640,16,16]{0,2,1:T(8,128)(2,1)} %param.22) | copy-start | bytes 983044
  185.0 41.1 %copy-start.9 = (bf16[16,16,864]{2,1,0:T(8,128)(2,1)S(1)}, bf16[16,16,864]{2,1,0:T(8,128)(2,1)}, u32[]{:S(2)}) copy-start(bf16[16,16,864]{2,1,0:T(8,128)(2,1)} %param.23) | copy-start | bytes 1327108
  196.4 2.5 copy-start.2
  294.5 44.3 %copy-start.4 = (bf16[576,640]{1,0:T(8,128)(2,1)S(1)}, bf16[576,640]{1,0:T(8,128)(2,1)}, u32[]{:S(2)}) copy-start(bf16[576,640]{1,0:T(8,128)(2,1)} %copy-done.3) | copy-start | bytes 2211844
  340.4 28.1 %copy-start.1 = (f32[8,3,5120]{2,0,1:T(8,128)S(1)}, f32[8,3,5120]{2,0,1:T(8,128)}, u32[]{:S(2)}) copy-start(f32[8,3,5120]{2,0,1:T(8,128)} %param.21) | copy-start | bytes 1474564
  341.8 23.4 %all-to-all-start = ((bf16[36,16,640]{2,0,1:T(8,128)(2,1)}), bf16[36,16,640]{2,0,1:T(8,128)(2,1)S(1)}, u32[]{:S(2)}, u32[]{:S(2)}) async-start(bf16[36,16,640]{2,0,1:T(8,128)(2,1)} %fusion.19), calls=%async_computation | async-start | bytes 1638400 | tf_op jit(solution)/shard_map/all_to_all | solution.py:222
Sparse Core Ops, SparseCore 0:
  9.5 52.4 all-gather.3
  78.9 42.8 reduce-scatter.6
  123.9 75.1 all-gather.5
  201.1 74.0 all-gather.7
  294.6 42.6 reduce-scatter.8
